TPU v7x, 512 devices: a whole 4x4x16 slice. The times are simulated.
512 devices in a mesh: dp: 128 (over y, z, core), mp: 4 (over x).
Axes of the slice: x: 4, y: 4, z: 16, core: 2. Of those that a mesh axis runs over, the one named last changes fastest.
Arguments:
- points: float32 [262144, 256], P('dp'), may hold values from -28 to 28
- residual: float32 [128, 262144], P('mp', 'dp'), may hold values from -6 to 6
- coeffs: float32 [128, 262144], P('mp', 'dp'), may hold values from -4 to 4
- block_index: int32 [512], replicated, may hold values from 0 to 262143, as said below
Outputs:
- new_residual: float32 [128, 262144], P('mp', 'dp')
- new_coeffs: float32 [128, 262144], P('mp', 'dp')
Inputs may be any that keep to these rules, and one draw needn't show every extreme that they name: `block_index`: distinct example indices; the 2048 examples of one index of dp hold at most 16 of them, and those of some index hold exactly 16.
All inputs are finite; a program needn't handle non-finite values.
Results may differ from a plain program's by a relative error of at most 0.00018.
Values sent between devices are 32-bit elements; how exact they have to be, the bound alone decides.
No kernel may reach another device: no remote copies, remote signals or barrier semaphores. Data moves between devices by JAX's collectives and lax.ppermute only.
A program may use at most 64 MiB of HBM per device.

v0:
```python
import jax
import jax.numpy as jnp
from jax import lax
from jax.sharding import Mesh
from jax.sharding import PartitionSpec as P
from jax.experimental import pallas as pl
from jax.experimental.pallas import tpu as pltpu

BLOCK = 512
MOST = 16


ridge_weight = 1.0

DP = ("y", "z", "c")


NB = 128
G = 8


def _dot_nt(a, b):
    return lax.dot_general(a, b, (((1,), (1,)), ((), ())), precision=lax.Precision.HIGHEST,
                           preferred_element_type=jnp.float32)


def _dot_nn(a, b):
    return lax.dot_general(a, b, (((1,), (0,)), ((), ())), precision=lax.Precision.HIGHEST,
                           preferred_element_type=jnp.float32)


def _dot_tn(a, b):
    return lax.dot_general(a, b, (((0,), (0,)), ((), ())), precision=lax.Precision.HIGHEST,
                           preferred_element_type=jnp.float32)


def _solve_kernel(a_ref, r_ref, x_ref, work, up, inv, dg):
    n = a_ref.shape[0]
    blocks = n // NB
    work[...] = a_ref[...]
    eye = (lax.broadcasted_iota(jnp.int32, (NB, NB), 0) == lax.broadcasted_iota(jnp.int32, (NB, NB), 1)).astype(jnp.float32)
    up[...] = jnp.zeros_like(up)
    lane = lax.broadcasted_iota(jnp.int32, (1, NB), 1)
    sub_g = lax.broadcasted_iota(jnp.int32, (G, 1), 0)
    lane_g = lax.broadcasted_iota(jnp.int32, (G, NB), 1)
    for b in range(blocks):
        r0 = b * NB
        dg[:, :NB] = work[r0:r0 + NB, r0:r0 + NB]
        dg[:, NB:] = eye

        def group(t, carry):
            g0 = pl.multiple_of(t * G, G)
            slab = dg[pl.ds(g0, G), :]
            for j in range(G):
                k = g0 + j
                row = slab[j:j + 1, :]
                c = jnp.sum(jnp.where(lane_g == g0 + sub_g, jnp.broadcast_to(row[:, :NB], (G, NB)), 0.0), axis=1, keepdims=True)
                scale = lax.rsqrt(c[j:j + 1, :])
                u = row * scale
                u_diag = jnp.where(lane >= k, u[:, :NB], 0.0)
                u = jnp.concatenate([u_diag, u[:, NB:]], axis=1)
                u_col = jnp.where(sub_g > j, c * scale, 0.0)
                slab = jnp.where(sub_g == j, u, slab - u_col * u)
            strip = dg[...]
            dg[...] = strip - _dot_tn(slab[:, :NB], slab)
            dg[pl.ds(g0, G), :] = slab
            return carry

        lax.fori_loop(0, NB // G, group, 0)
        up[r0:r0 + NB, r0:r0 + NB] = dg[:, :NB]
        inv[b] = dg[:, NB:]
        if b + 1 < blocks:
            panel = _dot_nn(inv[b], work[r0:r0 + NB, r0 + NB:n])
            up[r0:r0 + NB, r0 + NB:n] = panel
            work[r0 + NB:n, r0 + NB:n] -= _dot_tn(panel, panel)
    rhs = r_ref[...]
    z = []
    for b in range(blocks):
        acc = rhs[:, b * NB:(b + 1) * NB]
        for a in range(b):
            acc = acc - _dot_nn(z[a], up[a * NB:(a + 1) * NB, b * NB:(b + 1) * NB])
        z.append(_dot_nt(acc, inv[b]))
    x = [None] * blocks
    for b in reversed(range(blocks)):
        acc = z[b]
        for a in range(b + 1, blocks):
            acc = acc - _dot_nt(x[a], up[b * NB:(b + 1) * NB, a * NB:(a + 1) * NB])
        x[b] = _dot_nn(acc, inv[b])
    x_ref[...] = jnp.concatenate(x, axis=1)


def spd_solve(system, rhs, interpret=False):
    n = system.shape[0]
    return pl.pallas_call(
        _solve_kernel,
        out_shape=jax.ShapeDtypeStruct(rhs.shape, jnp.float32),
        scratch_shapes=[
            pltpu.VMEM((n, n), jnp.float32),
            pltpu.VMEM((n, n), jnp.float32),
            pltpu.VMEM((n // NB, NB, NB), jnp.float32),
            pltpu.VMEM((NB, 2 * NB), jnp.float32),
        ],
        interpret=interpret,
    )(system, rhs)


def on_device(points, residual, coeffs, block_index):
    highest = lax.Precision.HIGHEST
    shard_rows = points.shape[0]
    feature_count = points.shape[1]
    output_rows = residual.shape[0]
    y_count = lax.axis_size("y")
    z_count = lax.axis_size("z")
    c_count = lax.axis_size("c")
    dp_count = y_count * z_count * c_count
    position = (lax.axis_index("y") * z_count + lax.axis_index("z")) * c_count + lax.axis_index("c")
    owner_shard = block_index // shard_rows
    local_row = block_index - owner_shard * shard_rows
    mine = owner_shard == position
    own_squares = jnp.sum(points * points, axis=1)
    own_total = jnp.sum(own_squares)
    same_owner = owner_shard[:, None] == owner_shard[None, :]
    earlier = lax.broadcasted_iota(jnp.int32, (BLOCK, BLOCK), 1) < lax.broadcasted_iota(
        jnp.int32, (BLOCK, BLOCK), 0
    )
    slot_rank = jnp.sum((same_owner & earlier).astype(jnp.int32), axis=1)
    pick = mine[None, :] & (slot_rank[None, :] == lax.broadcasted_iota(jnp.int32, (MOST, BLOCK), 0))
    slot_row = jnp.sum(jnp.where(pick, local_row[None, :], 0), axis=1)
    slot_used = jnp.any(pick, axis=1)
    slot_points = jnp.where(slot_used[:, None], points[slot_row], 0.0)
    slot_resid = jnp.where(slot_used[:, None], residual[:, slot_row].T, 0.0)
    body = jnp.concatenate([slot_points, slot_resid], axis=1)
    extra = jnp.zeros((1, feature_count + output_rows), jnp.float32).at[0, 0].set(own_total)
    packed = jnp.concatenate([body, extra], axis=0)
    per_device = MOST + 1
    gathered = lax.all_gather(packed, "c", axis=0, tiled=True)
    gathered = lax.all_gather(gathered, "y", axis=0, tiled=True)
    gathered = lax.all_gather(gathered, "z", axis=0, tiled=True)
    owner_y = owner_shard // (z_count * c_count)
    owner_z = (owner_shard // c_count) % z_count
    owner_c = owner_shard % c_count
    owner_at = (owner_z * y_count + owner_y) * c_count + owner_c
    where_at = owner_at * per_device + slot_rank
    block_rows = gathered[where_at]
    block_points = block_rows[:, :feature_count]
    block_resid = block_rows[:, feature_count:].T
    square_total = jnp.sum(gathered.reshape(dp_count, per_device, -1)[:, MOST, 0])
    mean_sq = square_total / (shard_rows * dp_count)
    block_sq = jnp.sum(block_points * block_points, axis=1)
    inner_block = lax.dot_general(
        block_points,
        block_points,
        (((1,), (1,)), ((), ())),
        precision=highest,
        preferred_element_type=jnp.float32,
    )
    kernel_block = jnp.exp(-(block_sq[:, None] + block_sq[None, :] - 2.0 * inner_block) / mean_sq)
    system = kernel_block + ridge_weight * jnp.eye(BLOCK, dtype=jnp.float32)
    increment = spd_solve(system, block_resid)
    inner = lax.dot_general(
        block_points,
        points,
        (((1,), (1,)), ((), ())),
        precision=highest,
        preferred_element_type=jnp.float32,
    )
    weights = jnp.exp(-(block_sq[:, None] + own_squares[None, :] - 2.0 * inner) / mean_sq)
    change = jnp.dot(increment, weights, precision=highest, preferred_element_type=jnp.float32)
    column = jnp.where(mine, local_row, shard_rows)
    new_residual = (residual - change).at[:, column].add(-ridge_weight * increment, mode="drop")
    new_coeffs = coeffs.at[:, column].add(increment, mode="drop")
    return (new_residual, new_coeffs)


def solution(mesh):
    dp_parts = (4, mesh.shape["dp"] // 8, 2)
    split = Mesh(mesh.devices.reshape(dp_parts + (mesh.shape["mp"],)), DP + ("mp",))
    placed = (P(DP, None), P("mp", DP), P("mp", DP), P())
    return jax.shard_map(
        on_device,
        mesh=split,
        in_specs=placed,
        out_specs=(P("mp", DP), P("mp", DP)),
        check_vma=False,
    )
```

profile of v0, /device:TPU:24, one launch (start us, length us, event | category | flops | bytes accessed | tf_op | source)
XLA Modules:
  0.0 233.8 jit_solution(408630123705232281)
XLA Ops:
  7.9 0.7 compare_select_fusion
  9.1 1.3 copy.30
  10.4 2.8 %multiply_reduce_fusion = (f32[2048]{0:T(1024)S(1)}, f32[]{:T(128)}) fusion(f32[2048,256]{1,0:T(8,128)} %param.6), kind=kLoop, calls=%fused_computation.17 | loop fusion | flops 1570815 | bytes 2105348 | tf_op jit(solution)/shard_map/reduce_sum | solution.py:120
  13.1 2.2 gather_fusion
  17.3 1.9 all-gather
  19.2 14.6 %all-gather.1 = f32[4,34,288]{2,1,0:T(8,128)S(1)} all-gather(f32[1,34,288]{2,1,0:T(8,128)S(1)} %reshape.110), channel_id=1, replica_groups=mesh['y'=4,'z'=16,'c'=2,'mp'=4] {'y'}, dimensions={0}, use_global_device_ids=true | all-gather | bytes 195840 | tf_op jit(solution)/shard_map/all_gather | solution.py:137
  33.8 0.7 reshape.111
  34.5 1.4 copy.34
  35.9 76.6 %all-gather.4.cloned.1.call-done = f32[2176,288]{1,0:T(8,128)} async-done(((f32[136,288]{1,0:T(8,128)}), f32[2176,288]{1,0:T(8,128)}) %all-gather.4.cloned.1.call-update) | async-done | bytes 2506768 | tf_op jit(solution)/shard_map/all_gather | solution.py:138
  112.5 4.5 %gather_fusion.2 = f32[512,288]{1,0:T(8,128)} fusion(f32[2176,288]{1,0:T(8,128)} %all-gather.4.cloned.1.call-done, s32[1024]{0:T(1024)S(1)} %pad_clamp_fusion), kind=kCustom, calls=%fused_computation.2 | custom fusion | bytes 1181696 | tf_op jit(solution)/shard_map/gather | solution.py:144
  117.0 1.3 multiply_reduce_fusion.2
  118.3 1.7 slice.36
  120.0 7.3 %fusion.20 = f32[512,2048]{1,0:T(8,128)} fusion(f32[2048,256]{1,0:T(8,128)} %param.6, f32[512,288]{1,0:T(8,128)} %gather_fusion.2), kind=kOutput, calls=%fused_computation.30 | convolution fusion | flops 3221225472 | bytes 6815744 | tf_op jit(solution)/shard_map/dot_general | solution.py:160
  127.3 2.4 %reshape.64 = f32[128,17,288]{2,1,0:T(8,128)} reshape(f32[2176,288]{1,0:T(8,128)S(1)} %copy-done) | data formatting | bytes 5013504 | tf_op jit(solution)/shard_map/reshape | solution.py:147
  129.7 1.9 slice_reduce_fusion
  131.6 1.7 copy.38
  133.9 3.5 %fusion.18.a_ref = f32[512,512]{1,0:T(8,128)} fusion(f32[]{:T(128)S(6)} %div.56, f32[512]{0:T(512)S(1)} %multiply_reduce_fusion.2, f32[512,288]{1,0:T(8,128)} %gather_fusion.2), kind=kOutput, calls=%fused_computation.24 | convolution fusion | flops 807403520 | bytes 1576964 | tf_op jit(solution)/shard_map/dot_general | solution.py:150
  137.3 72.9 %shard_map.59 = f32[32,512]{1,0:T(8,128)} custom-call(f32[512,512]{1,0:T(8,128)} %fusion.18.a_ref, f32[32,512]{1,0:T(8,128)} %bitcast.14), custom_call_target="tpu_custom_call" | custom-call | tf_op jit(solution)/shard_map/pallas_call | solution.py:94
  210.3 0.8 multiply_bitcast_fusion
  211.2 5.7 %fusion.7 = f32[32,2048]{1,0:T(8,128)S(1)} fusion(f32[32,2048]{1,0:T(8,128)S(1)} %copy-done.4, f32[32,512]{1,0:T(8,128)} %shard_map.59, f32[512,2048]{1,0:T(8,128)} %fusion.20, f32[]{:T(128)S(6)} %div.56, f32[2048]{0:T(1024)S(1)} %get-tuple-element.22, f32[512]{0:T(512)S(1)} %multiply_reduce_fusion.2), kind=kOutput, calls=%fused_computation.12 | convolution fusion | flops 407961600 | bytes 4794372 | tf_op jit(solution)/shard_map/dot_general | solution.py:168
  217.3 3.7 %scatter_fusion = f32[32,2048]{0,1:T(8,128)S(1)} fusion(f32[32,2048]{0,1:T(8,128)S(1)} %copy.32, s32[512]{0:T(512)S(1)} %get-tuple-element.24, f32[512,32]{1,0:T(8,128)S(1)} %copy.33), kind=kCustom, calls=%fused_computation.3 | custom fusion | flops 16384 | bytes 198656 | tf_op jit(solution)/shard_map/scatter-add | solution.py:170
  221.0 1.0 copy.36
  222.2 3.7 %scatter_fusion.1 = f32[32,2048]{0,1:T(8,128)S(1)} fusion(f32[32,2048]{0,1:T(8,128)S(1)} %copy-done.1, s32[512]{0:T(512)S(1)} %get-tuple-element.24, f32[512,32]{1,0:T(8,128)S(1)} %copy.35), kind=kCustom, calls=%fused_computation.4 | custom fusion | flops 16384 | bytes 198656 | tf_op jit(solution)/shard_map/scatter-add | solution.py:171
  225.9 1.0 copy.37
  (28 shorter events, 2.6 us)
Async XLA Ops:
  7.2 27.3 %copy-start.3 = (f32[32,2048]{1,0:T(8,128)S(1)}, f32[32,2048]{1,0:T(8,128)}, u32[]{:S(2)}) copy-start(f32[32,2048]{1,0:T(8,128)} %param.8) | copy-start | bytes 786436
  7.2 105.4 %all-gather.4.cloned.1.call-start = ((), (), s32[]{:S(2)}) async-start(), calls=%async_computation | async-start | bytes 3551232 | tf_op jit(solution)/shard_map/all_gather | solution.py:138
  117.0 10.3 %copy-start = (f32[2176,288]{1,0:T(8,128)S(1)}, f32[2176,288]{1,0:T(8,128)}, u32[]{:S(2)}) copy-start(f32[2176,288]{1,0:T(8,128)} %all-gather.4.cloned.1.call-done) | copy-start | bytes 7520260
  129.7 81.4 %copy-start.4 = (f32[32,2048]{1,0:T(8,128)S(1)}, f32[32,2048]{1,0:T(8,128)}, u32[]{:S(2)}) copy-start(f32[32,2048]{1,0:T(8,128)} %param.7) | copy-start | bytes 786436
  211.1 10.9 %copy-start.2 = (f32[32,512]{1,0:T(8,128)S(1)}, f32[32,512]{1,0:T(8,128)}, u32[]{:S(2)}) copy-start(f32[32,512]{1,0:T(8,128)} %shard_map.59) | copy-start | bytes 196612
  216.9 5.3 %copy-start.1 = (f32[32,2048]{0,1:T(8,128)S(1)}, f32[32,2048]{0,1:T(8,128)}, u32[]{:S(2)}) copy-start(f32[32,2048]{0,1:T(8,128)} %copy.34) | copy-start | bytes 786436
Sparse Core Ops, SparseCore 0:
  34.6 77.8 all-gather.3
where the time goes:
time: 234 us
  waiting for transfers between devices  76.6 us (33%)
  Pallas kernels  72.9 us (31%)
  local copies, waits for them, and re-layouts  18.9 us (8%)
  matrix products  16.5 us (7%)
  blocking collectives  16.4 us (7%)
  other arithmetic  16.2 us (7%)
  between operations  16.1 us (7%)
    all_gather x1, waiting for transfers between devices, on_device(): gathered = lax.all_gather(gathered, 'z', axis=0, tiled=True)  76.6 us
    pallas_call x1, Pallas kernels, spd_solve(): pl.pallas_call(_solve_kernel, out_shape=jax.ShapeDtypeStruct(rhs.shape, j...  72.9 us
    all_gather x1, blocking collectives, on_device(): gathered = lax.all_gather(gathered, 'y', axis=0, tiled=True)  14.6 us
    dot_general x1, matrix products, on_device(): lax.dot_general(block_points, points, (((1,), (1,)), ((), ())), precision...  7.33 us
    unnamed x17, local copies, waits for them, and re-layouts  7.11 us
    dot_general x1, matrix products, on_device(): jnp.dot(increment, weights, precision=highest, preferred_element_type=jnp...  5.69 us
  transfers between devices with their start and end apart: 1, of which 1 were waited for; matrix products, arithmetic and copies ran while one was open for 1% of the time, Pallas kernels for 0%

commit v1 on v0

--- a/solution.py
+++ b/solution.py
@@ -127,10 +127,13 @@
     pick = mine[None, :] & (slot_rank[None, :] == lax.broadcasted_iota(jnp.int32, (MOST, BLOCK), 0))
     slot_row = jnp.sum(jnp.where(pick, local_row[None, :], 0), axis=1)
     slot_used = jnp.any(pick, axis=1)
-    slot_points = jnp.where(slot_used[:, None], points[slot_row], 0.0)
+    mp_count = lax.axis_size("mp")
+    share = feature_count // mp_count
+    slot_points = lax.dynamic_slice_in_dim(points[slot_row], lax.axis_index("mp") * share, share, 1)
+    slot_points = jnp.where(slot_used[:, None], slot_points, 0.0)
     slot_resid = jnp.where(slot_used[:, None], residual[:, slot_row].T, 0.0)
     body = jnp.concatenate([slot_points, slot_resid], axis=1)
-    extra = jnp.zeros((1, feature_count + output_rows), jnp.float32).at[0, 0].set(own_total)
+    extra = jnp.zeros((1, share + output_rows), jnp.float32).at[0, 0].set(own_total)
     packed = jnp.concatenate([body, extra], axis=0)
     per_device = MOST + 1
     gathered = lax.all_gather(packed, "c", axis=0, tiled=True)
@@ -142,8 +145,8 @@
     owner_at = (owner_z * y_count + owner_y) * c_count + owner_c
     where_at = owner_at * per_device + slot_rank
     block_rows = gathered[where_at]
-    block_points = block_rows[:, :feature_count]
-    block_resid = block_rows[:, feature_count:].T
+    block_points = lax.all_gather(block_rows[:, :share], "mp", axis=1, tiled=True)
+    block_resid = block_rows[:, share:].T
     square_total = jnp.sum(gathered.reshape(dp_count, per_device, -1)[:, MOST, 0])
     mean_sq = square_total / (shard_rows * dp_count)
     block_sq = jnp.sum(block_points * block_points, axis=1)

time: 234 us -> 183 us (0.78)
  waiting for transfers between devices: 76.6 us -> 0 us
  blocking collectives: 16.4 us -> 68.9 us
  between operations: 16.1 us -> 2.76 us
  local copies, waits for them, and re-layouts: 18.9 us -> 10.2 us
  matrix products: 16.5 us -> 12.8 us
    all_gather x1 -> x0, waiting for transfers between devices: 76.6 us -> none  [on_device(): gathered = lax.all_gather(gathered, 'z', axis=0, tiled=True)]
    all_gather x0 -> x2, blocking collectives: none -> 52.8 us  [the longest x1 39.7 us: on_device(): gathered = lax.all_gather(gathered, 'z', axis=0, tiled=True)]
    gather x1, local copies, waits for them, and re-layouts: 4.47 us -> 1.04 us  [on_device(): block_rows = gathered[where_at]]
    unnamed x17 -> x15, local copies, waits for them, and re-layouts: 7.11 us -> 4.4 us
  transfers between devices with their start and end apart: 1 -> 0, of which waited for: 1 -> 0; matrix products, arithmetic and copies ran while one was open for 1% -> 0% of each run, Pallas kernels for 0% -> 0%
where the time goes in v1:
time: 183 us; the launch traced here: 182 us
  Pallas kernels  72.9 us (40%)
  blocking collectives  68.9 us (38%)
  other arithmetic  14.5 us (8%)
  matrix products  12.8 us (7%)
  local copies, waits for them, and re-layouts  10.2 us (6%)
  between operations  2.76 us (2%)
    pallas_call x1, Pallas kernels, spd_solve(): pl.pallas_call(_solve_kernel, out_shape=jax.ShapeDtypeStruct(rhs.shape, j...  72.9 us
    all_gather x1, blocking collectives, on_device(): gathered = lax.all_gather(gathered, 'z', axis=0, tiled=True)  39.7 us
    all_gather x1, blocking collectives, on_device(): gathered = lax.all_gather(gathered, 'y', axis=0, tiled=True)  14.2 us
    all_gather x1, blocking collectives, on_device(): lax.all_gather(block_rows[:, :share], 'mp', axis=1, tiled=True)  13.1 us
    dot_general x1, matrix products, on_device(): lax.dot_general(block_points, points, (((1,), (1,)), ((), ())), precision...  7.05 us
    unnamed x15, local copies, waits for them, and re-layouts  4.4 us
    scatter-add x1, other arithmetic, on_device(): (residual - change).at[:, column]  3.91 us
    scatter-add x1, other arithmetic, on_device(): new_coeffs = coeffs.at[:, column].add(increment, mode='drop')  3.69 us

profile of v1, /device:TPU:24, one launch (start us, length us, event | category | flops | bytes accessed | tf_op | source)
XLA Modules:
  0.0 182.0 jit_solution(11638233971593173950)
XLA Ops:
  0.6 0.6 compare_reduce_fusion
  1.3 2.7 %multiply_reduce_fusion = (f32[2048]{0:T(1024)S(1)}, f32[]{:T(128)}) fusion(f32[2048,256]{1,0:T(8,128)} %param.6), kind=kLoop, calls=%fused_computation.17 | loop fusion | flops 1570815 | bytes 2105348 | tf_op jit(solution)/shard_map/reduce_sum | solution.py:120
  5.3 1.3 copy.31
  6.6 0.7 compare_select_fusion
  7.7 0.6 gather_fusion.1
  8.5 2.2 %gather_fusion = f32[16,256]{1,0:T(8,128)S(1)} fusion(f32[2048,256]{1,0:T(8,128)} %param.6, s32[1024]{0:T(1024)S(1)} %pad_clamp_fusion.1), kind=kCustom, calls=%fused_computation | custom fusion | bytes 32832 | tf_op jit(solution)/shard_map/gather | solution.py:132
  10.8 1.8 all-gather
  12.6 14.2 %all-gather.1 = f32[4,34,96]{2,1,0:T(8,128)S(1)} all-gather(f32[1,34,96]{2,1,0:T(8,128)S(1)} %reshape.110), channel_id=1, replica_groups=mesh['y'=4,'z'=16,'c'=2,'mp'=4] {'y'}, dimensions={0}, use_global_device_ids=true | all-gather | bytes 65280 | tf_op jit(solution)/shard_map/all_gather | solution.py:140
  26.9 39.7 %all_gather.14 = f32[2176,96]{1,0:T(8,128)S(1)} all-gather(f32[136,96]{1,0:T(8,128)S(1)} %reshape.111), channel_id=1, replica_groups=mesh['y'=4,'z'=16,'c'=2,'mp'=4] {'z'}, dimensions={0}, use_global_device_ids=true | all-gather | bytes 887808 | tf_op jit(solution)/shard_map/all_gather | solution.py:141
  66.6 1.0 gather_fusion.2
  67.7 13.1 %all_gather.15 = f32[512,256]{0,1:T(8,128)S(1)} all-gather(f32[512,64]{0,1:T(8,128)S(1)} %copy.32), channel_id=1, replica_groups=mesh['y'=4,'z'=16,'c'=2,'mp'=4] {'mp'}, dimensions={1}, use_global_device_ids=true | all-gather | bytes 655360 | tf_op jit(solution)/shard_map/all_gather | solution.py:148
  80.9 1.3 reshape.64
  82.1 1.9 %slice_reduce_fusion = f32[]{:T(128)} fusion(f32[128,17,96]{2,1,0:T(8,128)} %reshape.64), kind=kLoop, calls=%fused_computation.30 | loop fusion | flops 127 | bytes 516 | tf_op jit(solution)/shard_map/reduce_sum | solution.py:150
  84.8 2.3 %fusion.18.a_ref = f32[512,512]{1,0:T(8,128)} fusion(f32[512,256]{0,1:T(8,128)S(1)} %all_gather.15, f32[]{:T(128)S(6)} %div.56, f32[512]{0:T(512)S(1)} %multiply_reduce_fusion.2), kind=kOutput, calls=%fused_computation.24 | convolution fusion | flops 807403520 | bytes 1574916 | tf_op jit(solution)/shard_map/dot_general | solution.py:153
  87.2 0.7 copy.40
  87.9 72.9 %shard_map.59 = f32[32,512]{1,0:T(8,128)} custom-call(f32[512,512]{1,0:T(8,128)} %fusion.18.a_ref, f32[32,512]{1,0:T(8,128)} %bitcast.19), custom_call_target="tpu_custom_call" | custom-call | tf_op jit(solution)/shard_map/pallas_call | solution.py:94
  160.9 7.1 %fusion.36 = f32[512,2048]{1,0:T(8,128)S(1)} fusion(f32[512,256]{0,1:T(8,128)S(1)} %all_gather.15, f32[2048,256]{1,0:T(8,128)S(1)} %copy-done), kind=kOutput, calls=%fused_computation.79 | convolution fusion | flops 3221225472 | bytes 6815744 | tf_op jit(solution)/shard_map/dot_general | solution.py:163
  167.9 3.5 %fusion.7 = f32[32,2048]{1,0:T(8,128)S(1)} fusion(f32[32,2048]{1,0:T(8,128)S(1)} %copy-done.2, f32[32,512]{1,0:T(8,128)S(1)} %copy-done.1, f32[512,2048]{1,0:T(8,128)S(1)} %fusion.36, f32[]{:T(128)S(6)} %div.56, f32[2048]{0:T(1024)S(1)} %get-tuple-element.22, f32[512]{0:T(512)S(1)} %multiply_reduce_fusion.2), kind=kOutput, calls=%fused_computation.12 | convolution fusion | flops 407961600 | bytes 4794372 | tf_op jit(solution)/shard_map/dot_general | solution.py:171
  171.4 0.3 copy.34
  171.9 3.9 %scatter_fusion = f32[32,2048]{0,1:T(8,128)S(1)} fusion(f32[32,2048]{0,1:T(8,128)S(1)} %copy.34, s32[512]{0:T(512)S(1)} %get-tuple-element.24, f32[512,32]{1,0:T(8,128)S(1)} %copy.35), kind=kCustom, calls=%fused_computation.3 | custom fusion | flops 16384 | bytes 198656 | tf_op jit(solution)/shard_map/scatter-add | solution.py:173
  175.8 1.0 copy.38
  176.8 0.3 copy.36
  177.3 3.7 %scatter_fusion.1 = f32[32,2048]{0,1:T(8,128)S(1)} fusion(f32[32,2048]{0,1:T(8,128)S(1)} %copy.36, s32[512]{0:T(512)S(1)} %get-tuple-element.24, f32[512,32]{1,0:T(8,128)S(1)} %copy.37), kind=kCustom, calls=%fused_computation.4 | custom fusion | flops 16384 | bytes 198656 | tf_op jit(solution)/shard_map/scatter-add | solution.py:174
  181.0 1.0 copy.39
  (26 shorter events, 1.4 us)
Async XLA Ops:
  82.1 78.7 %copy-start = (f32[2048,256]{1,0:T(8,128)S(1)}, f32[2048,256]{1,0:T(8,128)}, u32[]{:S(2)}) copy-start(f32[2048,256]{1,0:T(8,128)} %param.6) | copy-start | bytes 6291460
  87.2 80.8 %copy-start.2 = (f32[32,2048]{1,0:T(8,128)S(1)}, f32[32,2048]{1,0:T(8,128)}, u32[]{:S(2)}) copy-start(f32[32,2048]{1,0:T(8,128)} %param.7) | copy-start | bytes 786436
  160.9 7.1 %copy-start.1 = (f32[32,512]{1,0:T(8,128)S(1)}, f32[32,512]{1,0:T(8,128)}, u32[]{:S(2)}) copy-start(f32[32,512]{1,0:T(8,128)} %shard_map.59) | copy-start | bytes 196612
  171.4 5.4 %copy-start.3 = (f32[32,2048]{1,0:T(8,128)S(1)}, f32[32,2048]{1,0:T(8,128)}, u32[]{:S(2)}) copy-start(f32[32,2048]{1,0:T(8,128)} %param.8) | copy-start | bytes 786436

commit v2 on v1

--- a/solution.py
+++ b/solution.py
@@ -16,7 +16,7 @@
 
 
 NB = 128
-G = 8
+G = 64
 
 
 def _dot_nt(a, b):

time: 183 us -> 165 us (0.902)
  Pallas kernels: 72.9 us -> 55.4 us
    pallas_call x1, Pallas kernels: 72.9 us -> 55.4 us  [spd_solve(): pl.pallas_call(_solve_kernel, out_shape=jax.ShapeDtypeStruct(rhs.shape, j...]
where the time goes in v2:
time: 165 us
  blocking collectives  68.9 us (42%)
  Pallas kernels  55.4 us (34%)
  other arithmetic  14.5 us (9%)
  matrix products  12.8 us (8%)
  local copies, waits for them, and re-layouts  10.2 us (6%)
  between operations  2.76 us (2%)
    pallas_call x1, Pallas kernels, spd_solve(): pl.pallas_call(_solve_kernel, out_shape=jax.ShapeDtypeStruct(rhs.shape, j...  55.4 us
    all_gather x1, blocking collectives, on_device(): gathered = lax.all_gather(gathered, 'z', axis=0, tiled=True)  39.7 us
    all_gather x1, blocking collectives, on_device(): gathered = lax.all_gather(gathered, 'y', axis=0, tiled=True)  14.2 us
    all_gather x1, blocking collectives, on_device(): lax.all_gather(block_rows[:, :share], 'mp', axis=1, tiled=True)  13.1 us
    dot_general x1, matrix products, on_device(): lax.dot_general(block_points, points, (((1,), (1,)), ((), ())), precision...  7.05 us
    unnamed x15, local copies, waits for them, and re-layouts  4.4 us
    scatter-add x1, other arithmetic, on_device(): (residual - change).at[:, column]  3.91 us
    scatter-add x1, other arithmetic, on_device(): new_coeffs = coeffs.at[:, column].add(increment, mode='drop')  3.69 us

profile of v2, /device:TPU:24, one launch (start us, length us, event | category | flops | bytes accessed | tf_op | source)
XLA Modules:
  0.0 164.5 jit_solution(15538174829788050383)
XLA Ops:
  0.6 0.6 compare_reduce_fusion
  1.3 2.7 %multiply_reduce_fusion = (f32[2048]{0:T(1024)S(1)}, f32[]{:T(128)}) fusion(f32[2048,256]{1,0:T(8,128)} %param.6), kind=kLoop, calls=%fused_computation.17 | loop fusion | flops 1570815 | bytes 2105348 | tf_op jit(solution)/shard_map/reduce_sum | solution.py:120
  5.3 1.3 copy.31
  6.6 0.7 compare_select_fusion
  7.7 0.6 gather_fusion.1
  8.5 2.2 %gather_fusion = f32[16,256]{1,0:T(8,128)S(1)} fusion(f32[2048,256]{1,0:T(8,128)} %param.6, s32[1024]{0:T(1024)S(1)} %pad_clamp_fusion.1), kind=kCustom, calls=%fused_computation | custom fusion | bytes 32832 | tf_op jit(solution)/shard_map/gather | solution.py:132
  10.8 1.8 %all-gather = f32[2,17,96]{2,1,0:T(8,128)S(1)} all-gather(f32[1,17,96]{2,1,0:T(8,128)S(1)} %fusion.22), channel_id=1, replica_groups=mesh['y'=4,'z'=16,'c'=2,'mp'=4] {'c'}, dimensions={0}, use_global_device_ids=true | all-gather | bytes 19584 | tf_op jit(solution)/shard_map/all_gather | solution.py:139
  12.6 14.2 %all-gather.1 = f32[4,34,96]{2,1,0:T(8,128)S(1)} all-gather(f32[1,34,96]{2,1,0:T(8,128)S(1)} %reshape.110), channel_id=1, replica_groups=mesh['y'=4,'z'=16,'c'=2,'mp'=4] {'y'}, dimensions={0}, use_global_device_ids=true | all-gather | bytes 65280 | tf_op jit(solution)/shard_map/all_gather | solution.py:140
  26.9 39.7 %all_gather.14 = f32[2176,96]{1,0:T(8,128)S(1)} all-gather(f32[136,96]{1,0:T(8,128)S(1)} %reshape.111), channel_id=1, replica_groups=mesh['y'=4,'z'=16,'c'=2,'mp'=4] {'z'}, dimensions={0}, use_global_device_ids=true | all-gather | bytes 887808 | tf_op jit(solution)/shard_map/all_gather | solution.py:141
  66.6 1.0 gather_fusion.2
  67.7 13.1 %all_gather.15 = f32[512,256]{0,1:T(8,128)S(1)} all-gather(f32[512,64]{0,1:T(8,128)S(1)} %copy.32), channel_id=1, replica_groups=mesh['y'=4,'z'=16,'c'=2,'mp'=4] {'mp'}, dimensions={1}, use_global_device_ids=true | all-gather | bytes 655360 | tf_op jit(solution)/shard_map/all_gather | solution.py:148
  80.9 1.3 reshape.64
  82.1 1.9 %slice_reduce_fusion = f32[]{:T(128)} fusion(f32[128,17,96]{2,1,0:T(8,128)} %reshape.64), kind=kLoop, calls=%fused_computation.30 | loop fusion | flops 127 | bytes 516 | tf_op jit(solution)/shard_map/reduce_sum | solution.py:150
  84.8 2.3 %fusion.18.a_ref = f32[512,512]{1,0:T(8,128)} fusion(f32[512,256]{0,1:T(8,128)S(1)} %all_gather.15, f32[]{:T(128)S(6)} %div.56, f32[512]{0:T(512)S(1)} %multiply_reduce_fusion.2), kind=kOutput, calls=%fused_computation.24 | convolution fusion | flops 807403520 | bytes 1574916 | tf_op jit(solution)/shard_map/dot_general | solution.py:153
  87.2 0.7 copy.40
  87.9 55.4 %shard_map.59 = f32[32,512]{1,0:T(8,128)} custom-call(f32[512,512]{1,0:T(8,128)} %fusion.18.a_ref, f32[32,512]{1,0:T(8,128)} %bitcast.19), custom_call_target="tpu_custom_call" | custom-call | tf_op jit(solution)/shard_map/pallas_call | solution.py:94
  143.3 7.1 %fusion.36 = f32[512,2048]{1,0:T(8,128)S(1)} fusion(f32[512,256]{0,1:T(8,128)S(1)} %all_gather.15, f32[2048,256]{1,0:T(8,128)S(1)} %copy-done), kind=kOutput, calls=%fused_computation.79 | convolution fusion | flops 3221225472 | bytes 6815744 | tf_op jit(solution)/shard_map/dot_general | solution.py:163
  150.4 3.5 %fusion.7 = f32[32,2048]{1,0:T(8,128)S(1)} fusion(f32[32,2048]{1,0:T(8,128)S(1)} %copy-done.2, f32[32,512]{1,0:T(8,128)S(1)} %copy-done.1, f32[512,2048]{1,0:T(8,128)S(1)} %fusion.36, f32[]{:T(128)S(6)} %div.56, f32[2048]{0:T(1024)S(1)} %get-tuple-element.22, f32[512]{0:T(512)S(1)} %multiply_reduce_fusion.2), kind=kOutput, calls=%fused_computation.12 | convolution fusion | flops 407961600 | bytes 4794372 | tf_op jit(solution)/shard_map/dot_general | solution.py:171
  153.9 0.3 copy.34
  154.4 3.9 %scatter_fusion = f32[32,2048]{0,1:T(8,128)S(1)} fusion(f32[32,2048]{0,1:T(8,128)S(1)} %copy.34, s32[512]{0:T(512)S(1)} %get-tuple-element.24, f32[512,32]{1,0:T(8,128)S(1)} %copy.35), kind=kCustom, calls=%fused_computation.3 | custom fusion | flops 16384 | bytes 198656 | tf_op jit(solution)/shard_map/scatter-add | solution.py:173
  158.3 1.0 copy.38
  159.3 0.3 copy.36
  159.8 3.7 %scatter_fusion.1 = f32[32,2048]{0,1:T(8,128)S(1)} fusion(f32[32,2048]{0,1:T(8,128)S(1)} %copy.36, s32[512]{0:T(512)S(1)} %get-tuple-element.24, f32[512,32]{1,0:T(8,128)S(1)} %copy.37), kind=kCustom, calls=%fused_computation.4 | custom fusion | flops 16384 | bytes 198656 | tf_op jit(solution)/shard_map/scatter-add | solution.py:174
  163.5 1.0 copy.39
  (26 shorter events, 1.4 us)
Async XLA Ops:
  82.1 61.2 %copy-start = (f32[2048,256]{1,0:T(8,128)S(1)}, f32[2048,256]{1,0:T(8,128)}, u32[]{:S(2)}) copy-start(f32[2048,256]{1,0:T(8,128)} %param.6) | copy-start | bytes 6291460
  87.2 63.2 %copy-start.2 = (f32[32,2048]{1,0:T(8,128)S(1)}, f32[32,2048]{1,0:T(8,128)}, u32[]{:S(2)}) copy-start(f32[32,2048]{1,0:T(8,128)} %param.7) | copy-start | bytes 786436
  143.3 7.1 %copy-start.1 = (f32[32,512]{1,0:T(8,128)S(1)}, f32[32,512]{1,0:T(8,128)}, u32[]{:S(2)}) copy-start(f32[32,512]{1,0:T(8,128)} %shard_map.59) | copy-start | bytes 196612
  153.9 5.4 %copy-start.3 = (f32[32,2048]{1,0:T(8,128)S(1)}, f32[32,2048]{1,0:T(8,128)}, u32[]{:S(2)}) copy-start(f32[32,2048]{1,0:T(8,128)} %param.8) | copy-start | bytes 786436

commit v3 on v2

--- a/solution.py
+++ b/solution.py
@@ -137,13 +137,9 @@
     packed = jnp.concatenate([body, extra], axis=0)
     per_device = MOST + 1
     gathered = lax.all_gather(packed, "c", axis=0, tiled=True)
+    gathered = lax.all_gather(gathered, "z", axis=0, tiled=True)
     gathered = lax.all_gather(gathered, "y", axis=0, tiled=True)
-    gathered = lax.all_gather(gathered, "z", axis=0, tiled=True)
-    owner_y = owner_shard // (z_count * c_count)
-    owner_z = (owner_shard // c_count) % z_count
-    owner_c = owner_shard % c_count
-    owner_at = (owner_z * y_count + owner_y) * c_count + owner_c
-    where_at = owner_at * per_device + slot_rank
+    where_at = owner_shard * per_device + slot_rank
     block_rows = gathered[where_at]
     block_points = lax.all_gather(block_rows[:, :share], "mp", axis=1, tiled=True)
     block_resid = block_rows[:, share:].T
@@ -170,8 +166,10 @@
     weights = jnp.exp(-(block_sq[:, None] + own_squares[None, :] - 2.0 * inner) / mean_sq)
     change = jnp.dot(increment, weights, precision=highest, preferred_element_type=jnp.float32)
     column = jnp.where(mine, local_row, shard_rows)
-    new_residual = (residual - change).at[:, column].add(-ridge_weight * increment, mode="drop")
-    new_coeffs = coeffs.at[:, column].add(increment, mode="drop")
+    placed = (column[:, None] == lax.broadcasted_iota(jnp.int32, (BLOCK, shard_rows), 1)).astype(jnp.float32)
+    spread = jnp.dot(increment, placed, precision=highest, preferred_element_type=jnp.float32)
+    new_residual = (residual - change) - ridge_weight * spread
+    new_coeffs = coeffs + spread
     return (new_residual, new_coeffs)
 
 

time: 165 us -> 156 us (0.945)
  other arithmetic: 14.5 us -> 6.82 us
  matrix products: 12.8 us -> 16.7 us
  blocking collectives: 68.9 us -> 65.8 us
  local copies, waits for them, and re-layouts: 10.2 us -> 7.86 us
    scatter-add x2 -> x0, other arithmetic: 7.6 us -> none  [the longest x1 3.91 us: on_device(): (residual - change).at[:, column]]
    dot_general x0 -> x1, matrix products: none -> 3.27 us  [on_device(): jnp.dot(increment, placed, precision=highest, preferred_element_type=jnp....]
    all_gather x1, blocking collectives: 39.7 us -> 37.2 us  [on_device(): gathered = lax.all_gather(gathered, 'z', axis=0, tiled=True)]
    unnamed x15 -> x13, local copies, waits for them, and re-layouts: 4.4 us -> 2.22 us
where the time goes in v3:
time: 156 us; the launch traced here: 155 us
  blocking collectives  65.8 us (42%)
  Pallas kernels  55.4 us (36%)
  matrix products  16.7 us (11%)
  local copies, waits for them, and re-layouts  7.86 us (5%)
  other arithmetic  6.82 us (4%)
  between operations  2.7 us (2%)
    pallas_call x1, Pallas kernels, spd_solve(): pl.pallas_call(_solve_kernel, out_shape=jax.ShapeDtypeStruct(rhs.shape, j...  55.4 us
    all_gather x1, blocking collectives, on_device(): gathered = lax.all_gather(gathered, 'z', axis=0, tiled=True)  37.2 us
    all_gather x1, blocking collectives, on_device(): gathered = lax.all_gather(gathered, 'y', axis=0, tiled=True)  13.7 us
    all_gather x1, blocking collectives, on_device(): lax.all_gather(block_rows[:, :share], 'mp', axis=1, tiled=True)  13.1 us
    dot_general x1, matrix products, on_device(): lax.dot_general(block_points, points, (((1,), (1,)), ((), ())), precision...  6.99 us
    dot_general x1, matrix products, on_device(): jnp.dot(increment, weights, precision=highest, preferred_element_type=jnp...  4.16 us
    dot_general x1, matrix products, on_device(): jnp.dot(increment, placed, precision=highest, preferred_element_type=jnp....  3.27 us

profile of v3, /device:TPU:24, one launch (start us, length us, event | category | flops | bytes accessed | tf_op | source)
XLA Modules:
  0.0 155.3 jit_solution(14503230082902942002)
XLA Ops:
  0.6 0.6 compare_reduce_fusion
  1.3 0.7 broadcast_select_fusion.1
  2.0 0.2 convert_reduce_fusion
  2.2 0.1 select_reduce_fusion
  2.3 0.1 fusion.26
  2.5 2.7 %multiply_reduce_fusion = (f32[2048]{0:T(1024)S(1)}, f32[]{:T(128)}) fusion(f32[2048,256]{1,0:T(8,128)} %param.6), kind=kLoop, calls=%fused_computation.19 | loop fusion | flops 1570815 | bytes 2105348 | tf_op jit(solution)/shard_map/reduce_sum | solution.py:120
  6.6 2.2 %gather_fusion = f32[16,256]{1,0:T(8,128)S(1)} fusion(f32[2048,256]{1,0:T(8,128)} %param.6, s32[1024]{0:T(1024)S(1)} %pad_clamp_fusion.1), kind=kCustom, calls=%fused_computation | custom fusion | bytes 32832 | tf_op jit(solution)/shard_map/gather | solution.py:132
  8.8 1.3 copy.16
  10.1 0.6 gather_fusion.1
  10.8 1.8 %all-gather = f32[2,17,96]{2,1,0:T(8,128)S(1)} all-gather(f32[1,17,96]{2,1,0:T(8,128)S(1)} %fusion.27), channel_id=1, replica_groups=mesh['y'=4,'z'=16,'c'=2,'mp'=4] {'c'}, dimensions={0}, use_global_device_ids=true | all-gather | bytes 19584 | tf_op jit(solution)/shard_map/all_gather | solution.py:139
  12.6 37.2 %all-gather.1 = f32[16,34,96]{2,1,0:T(8,128)S(1)} all-gather(f32[1,34,96]{2,1,0:T(8,128)S(1)} %reshape.93), channel_id=1, replica_groups=mesh['y'=4,'z'=16,'c'=2,'mp'=4] {'z'}, dimensions={0}, use_global_device_ids=true | all-gather | bytes 221952 | tf_op jit(solution)/shard_map/all_gather | solution.py:140
  49.9 0.2 copy.17
  50.0 13.7 %all-gather.2 = f32[4,544,96]{1,2,0:T(8,128)S(1)} all-gather(f32[1,544,96]{1,2,0:T(8,128)S(1)} %copy.17), channel_id=1, replica_groups=mesh['y'=4,'z'=16,'c'=2,'mp'=4] {'y'}, dimensions={0}, use_global_device_ids=true | all-gather | bytes 1044480 | tf_op jit(solution)/shard_map/all_gather | solution.py:141
  63.7 0.4 copy.18
  64.1 1.0 gather_fusion.2
  65.4 0.7 copy.22
  66.2 13.1 %all_gather.15 = f32[512,256]{0,1:T(8,128)S(1)} all-gather(f32[512,64]{0,1:T(8,128)S(1)} %copy.19), channel_id=1, replica_groups=mesh['y'=4,'z'=16,'c'=2,'mp'=4] {'mp'}, dimensions={1}, use_global_device_ids=true | all-gather | bytes 655360 | tf_op jit(solution)/shard_map/all_gather | solution.py:144
  79.3 1.3 reshape.65
  80.6 1.9 %slice_reduce_fusion = f32[]{:T(128)} fusion(f32[128,17,96]{2,1,0:T(8,128)} %reshape.65), kind=kLoop, calls=%fused_computation.32 | loop fusion | flops 127 | bytes 516 | tf_op jit(solution)/shard_map/reduce_sum | solution.py:146
  83.2 2.3 %fusion.23.a_ref = f32[512,512]{1,0:T(8,128)} fusion(f32[512,256]{0,1:T(8,128)S(1)} %all_gather.15, f32[]{:T(128)S(6)} %div.31, f32[512]{0:T(512)S(1)} %multiply_reduce_fusion.2), kind=kOutput, calls=%fused_computation.26 | convolution fusion | flops 807403520 | bytes 1574916 | tf_op jit(solution)/shard_map/dot_general | solution.py:149
  85.4 55.4 %shard_map.59 = f32[32,512]{1,0:T(8,128)} custom-call(f32[512,512]{1,0:T(8,128)} %fusion.23.a_ref, f32[32,512]{1,0:T(8,128)} %bitcast.18), custom_call_target="tpu_custom_call" | custom-call | tf_op jit(solution)/shard_map/pallas_call | solution.py:94
  140.9 3.3 %fusion.32 = (f32[32,2048]{1,0:T(8,128)}, f32[32,2048]{1,0:T(8,128)S(1)}) fusion(f32[32,2048]{1,0:T(8,128)S(1)} %copy-done.3, f32[32,512]{1,0:T(8,128)} %shard_map.59, s32[512]{0:T(512)S(1)} %get-tuple-element.16), kind=kOutput, calls=%fused_computation.59 | convolution fusion | flops 403767296 | bytes 854016 | tf_op jit(solution)/shard_map/dot_general | solution.py:170
  144.1 7.0 %fusion.33 = f32[512,2048]{1,0:T(8,128)S(1)} fusion(f32[512,256]{0,1:T(8,128)S(1)} %all_gather.15, f32[2048,256]{1,0:T(8,128)S(1)} %copy-done), kind=kOutput, calls=%fused_computation.60 | convolution fusion | flops 3221225472 | bytes 6815744 | tf_op jit(solution)/shard_map/dot_general | solution.py:159
  151.2 4.2 %fusion.11 = f32[32,2048]{1,0:T(8,128)} fusion(f32[32,2048]{1,0:T(8,128)S(1)} %get-tuple-element.21, f32[32,2048]{1,0:T(8,128)S(1)} %copy-done.1, f32[32,512]{1,0:T(8,128)S(1)} %copy-done.2, f32[512,2048]{1,0:T(8,128)S(1)} %fusion.33, f32[]{:T(128)S(6)} %div.31, f32[2048]{0:T(1024)S(1)} %get-tuple-element.14, f32[512]{0:T(512)S(1)} %multiply_reduce_fusion.2), kind=kOutput, calls=%fused_computation.13 | convolution fusion | flops 408027136 | bytes 5056516 | tf_op jit(solution)/shard_map/dot_general | solution.py:167
  (20 shorter events, 0.6 us)
Async XLA Ops:
  79.3 61.5 %copy-start.3 = (f32[32,2048]{1,0:T(8,128)S(1)}, f32[32,2048]{1,0:T(8,128)}, u32[]{:S(2)}) copy-start(f32[32,2048]{1,0:T(8,128)} %param.8) | copy-start | bytes 786436
  80.6 63.5 %copy-start = (f32[2048,256]{1,0:T(8,128)S(1)}, f32[2048,256]{1,0:T(8,128)}, u32[]{:S(2)}) copy-start(f32[2048,256]{1,0:T(8,128)} %param.6) | copy-start | bytes 6291460
  140.9 10.3 %copy-start.1 = (f32[32,2048]{1,0:T(8,128)S(1)}, f32[32,2048]{1,0:T(8,128)}, u32[]{:S(2)}) copy-start(f32[32,2048]{1,0:T(8,128)} %param.7) | copy-start | bytes 786436
  140.9 10.3 %copy-start.2 = (f32[32,512]{1,0:T(8,128)S(1)}, f32[32,512]{1,0:T(8,128)}, u32[]{:S(2)}) copy-start(f32[32,512]{1,0:T(8,128)} %shard_map.59) | copy-start | bytes 196612

commit v4 on v3

--- a/solution.py
+++ b/solution.py
@@ -16,7 +16,7 @@
 
 
 NB = 128
-G = 64
+G = 128
 
 
 def _dot_nt(a, b):

time: 156 us -> 155 us (level)
  Pallas kernels: 55.4 us -> 53.7 us
    pallas_call x1, Pallas kernels: 55.4 us -> 53.7 us  [spd_solve(): pl.pallas_call(_solve_kernel, out_shape=jax.ShapeDtypeStruct(rhs.shape, j...]
where the time goes in v4:
time: 155 us; the launch traced here: 154 us
  blocking collectives  66 us (43%)
  Pallas kernels  53.7 us (35%)
  matrix products  16.9 us (11%)
  local copies, waits for them, and re-layouts  7.86 us (5%)
  other arithmetic  6.82 us (4%)
  between operations  2.7 us (2%)
    pallas_call x1, Pallas kernels, spd_solve(): pl.pallas_call(_solve_kernel, out_shape=jax.ShapeDtypeStruct(rhs.shape, j...  53.7 us
    all_gather x1, blocking collectives, on_device(): gathered = lax.all_gather(gathered, 'z', axis=0, tiled=True)  37.2 us
    all_gather x1, blocking collectives, on_device(): gathered = lax.all_gather(gathered, 'y', axis=0, tiled=True)  13.7 us
    all_gather x1, blocking collectives, on_device(): lax.all_gather(block_rows[:, :share], 'mp', axis=1, tiled=True)  13.3 us
    dot_general x1, matrix products, on_device(): lax.dot_general(block_points, points, (((1,), (1,)), ((), ())), precision...  7.25 us
    dot_general x1, matrix products, on_device(): jnp.dot(increment, weights, precision=highest, preferred_element_type=jnp...  4.16 us
    dot_general x1, matrix products, on_device(): jnp.dot(increment, placed, precision=highest, preferred_element_type=jnp....  3.27 us

profile of v4, /device:TPU:24, one launch (start us, length us, event | category | flops | bytes accessed | tf_op | source)
XLA Modules:
  0.0 154.1 jit_solution(2206792214712668273)
XLA Ops:
  0.6 0.6 compare_reduce_fusion
  1.3 0.7 broadcast_select_fusion.1
  2.0 0.2 convert_reduce_fusion
  2.2 0.1 select_reduce_fusion
  2.3 0.1 fusion.26
  2.5 2.7 %multiply_reduce_fusion = (f32[2048]{0:T(1024)S(1)}, f32[]{:T(128)}) fusion(f32[2048,256]{1,0:T(8,128)} %param.6), kind=kLoop, calls=%fused_computation.19 | loop fusion | flops 1570815 | bytes 2105348 | tf_op jit(solution)/shard_map/reduce_sum | solution.py:120
  6.6 2.2 %gather_fusion = f32[16,256]{1,0:T(8,128)S(1)} fusion(f32[2048,256]{1,0:T(8,128)} %param.6, s32[1024]{0:T(1024)S(1)} %pad_clamp_fusion.1), kind=kCustom, calls=%fused_computation | custom fusion | bytes 32832 | tf_op jit(solution)/shard_map/gather | solution.py:132
  8.8 1.3 copy.16
  10.1 0.6 gather_fusion.1
  10.8 1.8 %all-gather = f32[2,17,96]{2,1,0:T(8,128)S(1)} all-gather(f32[1,17,96]{2,1,0:T(8,128)S(1)} %fusion.27), channel_id=1, replica_groups=mesh['y'=4,'z'=16,'c'=2,'mp'=4] {'c'}, dimensions={0}, use_global_device_ids=true | all-gather | bytes 19584 | tf_op jit(solution)/shard_map/all_gather | solution.py:139
  12.6 37.2 %all-gather.1 = f32[16,34,96]{2,1,0:T(8,128)S(1)} all-gather(f32[1,34,96]{2,1,0:T(8,128)S(1)} %reshape.93), channel_id=1, replica_groups=mesh['y'=4,'z'=16,'c'=2,'mp'=4] {'z'}, dimensions={0}, use_global_device_ids=true | all-gather | bytes 221952 | tf_op jit(solution)/shard_map/all_gather | solution.py:140
  49.9 0.2 copy.17
  50.0 13.7 %all-gather.2 = f32[4,544,96]{1,2,0:T(8,128)S(1)} all-gather(f32[1,544,96]{1,2,0:T(8,128)S(1)} %copy.17), channel_id=1, replica_groups=mesh['y'=4,'z'=16,'c'=2,'mp'=4] {'y'}, dimensions={0}, use_global_device_ids=true | all-gather | bytes 1044480 | tf_op jit(solution)/shard_map/all_gather | solution.py:141
  63.7 0.4 copy.18
  64.1 1.0 gather_fusion.2
  65.4 0.7 copy.22
  66.2 13.3 %all_gather.15 = f32[512,256]{0,1:T(8,128)S(1)} all-gather(f32[512,64]{0,1:T(8,128)S(1)} %copy.19), channel_id=1, replica_groups=mesh['y'=4,'z'=16,'c'=2,'mp'=4] {'mp'}, dimensions={1}, use_global_device_ids=true | all-gather | bytes 655360 | tf_op jit(solution)/shard_map/all_gather | solution.py:144
  79.5 1.3 reshape.65
  80.8 1.9 %slice_reduce_fusion = f32[]{:T(128)} fusion(f32[128,17,96]{2,1,0:T(8,128)} %reshape.65), kind=kLoop, calls=%fused_computation.32 | loop fusion | flops 127 | bytes 516 | tf_op jit(solution)/shard_map/reduce_sum | solution.py:146
  83.4 2.3 %fusion.23.a_ref = f32[512,512]{1,0:T(8,128)} fusion(f32[512,256]{0,1:T(8,128)S(1)} %all_gather.15, f32[]{:T(128)S(6)} %div.31, f32[512]{0:T(512)S(1)} %multiply_reduce_fusion.2), kind=kOutput, calls=%fused_computation.26 | convolution fusion | flops 807403520 | bytes 1574916 | tf_op jit(solution)/shard_map/dot_general | solution.py:149
  85.6 53.7 %shard_map.59 = f32[32,512]{1,0:T(8,128)} custom-call(f32[512,512]{1,0:T(8,128)} %fusion.23.a_ref, f32[32,512]{1,0:T(8,128)} %bitcast.18), custom_call_target="tpu_custom_call" | custom-call | tf_op jit(solution)/shard_map/pallas_call | solution.py:94
  139.4 3.3 %fusion.32 = (f32[32,2048]{1,0:T(8,128)}, f32[32,2048]{1,0:T(8,128)S(1)}) fusion(f32[32,2048]{1,0:T(8,128)S(1)} %copy-done.3, f32[32,512]{1,0:T(8,128)} %shard_map.59, s32[512]{0:T(512)S(1)} %get-tuple-element.16), kind=kOutput, calls=%fused_computation.59 | convolution fusion | flops 403767296 | bytes 854016 | tf_op jit(solution)/shard_map/dot_general | solution.py:170
  142.6 7.2 %fusion.33 = f32[512,2048]{1,0:T(8,128)S(1)} fusion(f32[512,256]{0,1:T(8,128)S(1)} %all_gather.15, f32[2048,256]{1,0:T(8,128)S(1)} %copy-done), kind=kOutput, calls=%fused_computation.60 | convolution fusion | flops 3221225472 | bytes 6815744 | tf_op jit(solution)/shard_map/dot_general | solution.py:159
  149.9 4.2 %fusion.11 = f32[32,2048]{1,0:T(8,128)} fusion(f32[32,2048]{1,0:T(8,128)S(1)} %get-tuple-element.21, f32[32,2048]{1,0:T(8,128)S(1)} %copy-done.1, f32[32,512]{1,0:T(8,128)S(1)} %copy-done.2, f32[512,2048]{1,0:T(8,128)S(1)} %fusion.33, f32[]{:T(128)S(6)} %div.31, f32[2048]{0:T(1024)S(1)} %get-tuple-element.14, f32[512]{0:T(512)S(1)} %multiply_reduce_fusion.2), kind=kOutput, calls=%fused_computation.13 | convolution fusion | flops 408027136 | bytes 5056516 | tf_op jit(solution)/shard_map/dot_general | solution.py:167
  (20 shorter events, 0.6 us)
Async XLA Ops:
  79.5 59.8 %copy-start.3 = (f32[32,2048]{1,0:T(8,128)S(1)}, f32[32,2048]{1,0:T(8,128)}, u32[]{:S(2)}) copy-start(f32[32,2048]{1,0:T(8,128)} %param.8) | copy-start | bytes 786436
  80.8 61.9 %copy-start = (f32[2048,256]{1,0:T(8,128)S(1)}, f32[2048,256]{1,0:T(8,128)}, u32[]{:S(2)}) copy-start(f32[2048,256]{1,0:T(8,128)} %param.6) | copy-start | bytes 6291460
  139.4 10.5 %copy-start.1 = (f32[32,2048]{1,0:T(8,128)S(1)}, f32[32,2048]{1,0:T(8,128)}, u32[]{:S(2)}) copy-start(f32[32,2048]{1,0:T(8,128)} %param.7) | copy-start | bytes 786436
  139.4 10.5 %copy-start.2 = (f32[32,512]{1,0:T(8,128)S(1)}, f32[32,512]{1,0:T(8,128)}, u32[]{:S(2)}) copy-start(f32[32,512]{1,0:T(8,128)} %shard_map.59) | copy-start | bytes 196612

commit v5 on v4

--- a/solution.py
+++ b/solution.py
@@ -34,10 +34,14 @@
                            preferred_element_type=jnp.float32)
 
 
-def _solve_kernel(a_ref, r_ref, x_ref, work, up, inv, dg):
-    n = a_ref.shape[0]
+def _solve_kernel(p_ref, sq_col_ref, sq_row_ref, m_ref, r_ref, x_ref, work, up, inv, dg):
+    n = p_ref.shape[0]
     blocks = n // NB
-    work[...] = a_ref[...]
+    p = p_ref[...]
+    inner = _dot_nt(p, p)
+    kern = jnp.exp(-(sq_col_ref[...] + sq_row_ref[...] - 2.0 * inner) / m_ref[...])
+    on_diag = lax.broadcasted_iota(jnp.int32, (n, n), 0) == lax.broadcasted_iota(jnp.int32, (n, n), 1)
+    work[...] = jnp.where(on_diag, kern + ridge_weight, kern)
     eye = (lax.broadcasted_iota(jnp.int32, (NB, NB), 0) == lax.broadcasted_iota(jnp.int32, (NB, NB), 1)).astype(jnp.float32)
     up[...] = jnp.zeros_like(up)
     lane = lax.broadcasted_iota(jnp.int32, (1, NB), 1)
@@ -89,8 +93,8 @@
     x_ref[...] = jnp.concatenate(x, axis=1)
 
 
-def spd_solve(system, rhs, interpret=False):
-    n = system.shape[0]
+def spd_solve(block_points, block_sq, mean_sq, rhs, interpret=False):
+    n = block_points.shape[0]
     return pl.pallas_call(
         _solve_kernel,
         out_shape=jax.ShapeDtypeStruct(rhs.shape, jnp.float32),
@@ -101,7 +105,7 @@
             pltpu.VMEM((NB, 2 * NB), jnp.float32),
         ],
         interpret=interpret,
-    )(system, rhs)
+    )(block_points, block_sq[:, None], block_sq[None, :], jnp.reshape(mean_sq, (1, 1)), rhs)
 
 
 def on_device(points, residual, coeffs, block_index):
@@ -146,16 +150,7 @@
     square_total = jnp.sum(gathered.reshape(dp_count, per_device, -1)[:, MOST, 0])
     mean_sq = square_total / (shard_rows * dp_count)
     block_sq = jnp.sum(block_points * block_points, axis=1)
-    inner_block = lax.dot_general(
-        block_points,
-        block_points,
-        (((1,), (1,)), ((), ())),
-        precision=highest,
-        preferred_element_type=jnp.float32,
-    )
-    kernel_block = jnp.exp(-(block_sq[:, None] + block_sq[None, :] - 2.0 * inner_block) / mean_sq)
-    system = kernel_block + ridge_weight * jnp.eye(BLOCK, dtype=jnp.float32)
-    increment = spd_solve(system, block_resid)
+    increment = spd_solve(block_points, block_sq, mean_sq, block_resid)
     inner = lax.dot_general(
         block_points,
         points,

time: 155 us -> 161 us (1.039)
  local copies, waits for them, and re-layouts: 7.86 us -> 13.9 us
    dot_general x1 -> x0, matrix products: 2.26 us -> none  [on_device(): lax.dot_general(block_points, block_points, (((1,), (1,)), ((), ())), pre...]
    all_gather x0 -> x1, local copies, waits for them, and re-layouts: none -> 2.04 us  [on_device(): lax.all_gather(block_rows[:, :share], 'mp', axis=1, tiled=True)]
    unnamed x13 -> x17, local copies, waits for them, and re-layouts: 2.22 us -> 3.96 us
where the time goes in v5:
time: 161 us; the launch traced here: 160 us
  blocking collectives  66.2 us (41%)
  Pallas kernels  54.5 us (34%)
  matrix products  15.8 us (10%)
  local copies, waits for them, and re-layouts  13.9 us (9%)
  other arithmetic  6.68 us (4%)
  between operations  2.7 us (2%)
    pallas_call x1, Pallas kernels, spd_solve(): pl.pallas_call(_solve_kernel, out_shape=jax.ShapeDtypeStruct(rhs.shape, j...  54.5 us
    all_gather x1, blocking collectives, on_device(): gathered = lax.all_gather(gathered, 'z', axis=0, tiled=True)  37.2 us
    all_gather x1, blocking collectives, on_device(): gathered = lax.all_gather(gathered, 'y', axis=0, tiled=True)  13.7 us
    all_gather x1, blocking collectives, on_device(): lax.all_gather(block_rows[:, :share], 'mp', axis=1, tiled=True)  13.5 us
    dot_general x1, matrix products, on_device(): lax.dot_general(block_points, points, (((1,), (1,)), ((), ())), precision...  8.28 us
    dot_general x1, matrix products, on_device(): jnp.dot(increment, weights, precision=highest, preferred_element_type=jnp...  4.16 us
    unnamed x17, local copies, waits for them, and re-layouts  3.96 us
    dot_general x1, matrix products, on_device(): jnp.dot(increment, placed, precision=highest, preferred_element_type=jnp....  3.39 us

profile of v5, /device:TPU:24, one launch (start us, length us, event | category | flops | bytes accessed | tf_op | source)
XLA Modules:
  0.0 159.8 jit_solution(3740194456385772222)
XLA Ops:
  0.6 0.6 compare_reduce_fusion
  1.3 0.7 broadcast_select_fusion.1
  2.5 2.7 %multiply_reduce_fusion = (f32[2048]{0:T(1024)S(1)}, f32[]{:T(128)}) fusion(f32[2048,256]{1,0:T(8,128)} %param.6), kind=kLoop, calls=%fused_computation.19 | loop fusion | flops 1570815 | bytes 2105348 | tf_op jit(solution)/shard_map/reduce_sum | solution.py:124
  6.6 2.2 %gather_fusion = f32[16,256]{1,0:T(8,128)S(1)} fusion(f32[2048,256]{1,0:T(8,128)} %param.6, s32[1024]{0:T(1024)S(1)} %pad_clamp_fusion.1), kind=kCustom, calls=%fused_computation | custom fusion | bytes 32832 | tf_op jit(solution)/shard_map/gather | solution.py:136
  8.8 1.3 copy.19
  10.1 0.6 gather_fusion.1
  10.8 1.8 %all-gather = f32[2,17,96]{2,1,0:T(8,128)S(1)} all-gather(f32[1,17,96]{2,1,0:T(8,128)S(1)} %fusion.22), channel_id=1, replica_groups=mesh['y'=4,'z'=16,'c'=2,'mp'=4] {'c'}, dimensions={0}, use_global_device_ids=true | all-gather | bytes 19584 | tf_op jit(solution)/shard_map/all_gather | solution.py:143
  12.6 37.2 %all-gather.1 = f32[16,34,96]{2,1,0:T(8,128)S(1)} all-gather(f32[1,34,96]{2,1,0:T(8,128)S(1)} %reshape.96), channel_id=1, replica_groups=mesh['y'=4,'z'=16,'c'=2,'mp'=4] {'z'}, dimensions={0}, use_global_device_ids=true | all-gather | bytes 221952 | tf_op jit(solution)/shard_map/all_gather | solution.py:144
  50.0 13.7 %all-gather.2 = f32[4,544,96]{1,2,0:T(8,128)S(1)} all-gather(f32[1,544,96]{1,2,0:T(8,128)S(1)} %copy.20), channel_id=1, replica_groups=mesh['y'=4,'z'=16,'c'=2,'mp'=4] {'y'}, dimensions={0}, use_global_device_ids=true | all-gather | bytes 1044480 | tf_op jit(solution)/shard_map/all_gather | solution.py:145
  63.7 0.4 copy.21
  64.1 1.0 gather_fusion.2
  65.2 0.8 copy.22
  65.9 0.8 slice.36
  66.8 1.7 %copy.27 = f32[512,32]{0,1:T(8,128)} copy(f32[512,32]{1,0:T(8,128)} %slice.36) | data formatting | bytes 131072
  68.4 13.5 %all_gather.15 = f32[512,256]{0,1:T(8,128)S(1)} all-gather(f32[512,64]{0,1:T(8,128)} %copy.22), channel_id=1, replica_groups=mesh['y'=4,'z'=16,'c'=2,'mp'=4] {'mp'}, dimensions={1}, use_global_device_ids=true | all-gather | bytes 655360 | tf_op jit(solution)/shard_map/all_gather | solution.py:148
  82.0 0.8 copy-done.1
  82.8 0.9 copy.26.sq_col_ref
  83.7 2.0 %copy.25.p_ref = f32[512,256]{1,0:T(8,128)} copy(f32[512,256]{0,1:T(8,128)} %copy-done.1) | data formatting | bytes 1048576 | tf_op jit(solution)/shard_map/all_gather | solution.py:148
  85.7 1.3 reshape.67
  87.0 1.8 %slice_reduce_fusion = f32[]{:T(128)} fusion(f32[128,17,96]{2,1,0:T(8,128)} %reshape.67), kind=kLoop, calls=%fused_computation.25 | loop fusion | flops 127 | bytes 516 | tf_op jit(solution)/shard_map/reduce_sum | solution.py:150
  89.4 54.5 %shard_map.59 = f32[32,512]{1,0:T(8,128)} custom-call(f32[512,256]{1,0:T(8,128)} %copy.25.p_ref, f32[512,1]{1,0:T(8,128)} %copy.26.sq_col_ref, f32[1,512]{1,0:T(1,128)} %bitcast.21, f32[1,1]{1,0:T(1,128)} %bitcast.7.m_ref, f32[32,512]{1,0:T(8,128)} %bitcast.19), custom_call_target="tpu_custom_call" | custom-call | tf_op jit(solution)/shard_map/pallas_call | solution.py:98
  144.0 3.4 %fusion.27 = (f32[32,2048]{1,0:T(8,128)}, f32[32,2048]{1,0:T(8,128)S(1)}) fusion(f32[32,2048]{1,0:T(8,128)} %param.8, f32[32,512]{1,0:T(8,128)} %shard_map.59, s32[512]{0:T(512)S(1)} %get-tuple-element.16), kind=kOutput, calls=%fused_computation.52 | convolution fusion | flops 403767296 | bytes 854016 | tf_op jit(solution)/shard_map/dot_general | solution.py:165
  147.3 8.3 %fusion.28 = f32[512,2048]{1,0:T(8,128)S(1)} fusion(f32[512,256]{0,1:T(8,128)} %copy-done.1, f32[2048,256]{1,0:T(8,128)S(1)} %copy-done), kind=kOutput, calls=%fused_computation.53 | convolution fusion | flops 3221225472 | bytes 6815744 | tf_op jit(solution)/shard_map/dot_general | solution.py:154
  155.7 4.2 %fusion.11 = f32[32,2048]{1,0:T(8,128)} fusion(f32[32,2048]{1,0:T(8,128)S(1)} %get-tuple-element.21, f32[32,2048]{1,0:T(8,128)S(1)} %copy-done.2, f32[32,512]{1,0:T(8,128)S(1)} %copy-done.3, f32[512,2048]{1,0:T(8,128)S(1)} %fusion.28, f32[]{:T(128)} %div.25, f32[2048]{0:T(1024)S(1)} %get-tuple-element.14, f32[512]{0:T(512)S(1)} %copy-done.5), kind=kOutput, calls=%fused_computation.13 | convolution fusion | flops 408027136 | bytes 5056516 | tf_op jit(solution)/shard_map/dot_general | solution.py:162
  (25 shorter events, 1.0 us)
Async XLA Ops:
  65.9 81.4 %copy-start = (f32[2048,256]{1,0:T(8,128)S(1)}, f32[2048,256]{1,0:T(8,128)}, u32[]{:S(2)}) copy-start(f32[2048,256]{1,0:T(8,128)} %param.6) | copy-start | bytes 6291460
  82.0 0.8 copy-start.1
  82.8 6.6 %copy-start.4 = (f32[512]{0:T(512)}, f32[512]{0:T(512)S(1)}, u32[]{:S(2)}) copy-start(f32[512]{0:T(512)S(1)} %multiply_reduce_fusion.2) | copy-start | bytes 6148
  144.0 11.7 %copy-start.2 = (f32[32,2048]{1,0:T(8,128)S(1)}, f32[32,2048]{1,0:T(8,128)}, u32[]{:S(2)}) copy-start(f32[32,2048]{1,0:T(8,128)} %param.7) | copy-start | bytes 786436
  144.0 11.7 %copy-start.3 = (f32[32,512]{1,0:T(8,128)S(1)}, f32[32,512]{1,0:T(8,128)}, u32[]{:S(2)}) copy-start(f32[32,512]{1,0:T(8,128)} %shard_map.59) | copy-start | bytes 196612
  144.0 11.7 %copy-start.5 = (f32[512]{0:T(512)S(1)}, f32[512]{0:T(512)}, u32[]{:S(2)}) copy-start(f32[512]{0:T(512)} %copy-done.4) | copy-start | bytes 6148

commit v6 on v4

--- a/solution.py
+++ b/solution.py
@@ -37,15 +37,14 @@
 def _solve_kernel(a_ref, r_ref, x_ref, work, up, inv, dg):
     n = a_ref.shape[0]
     blocks = n // NB
-    work[...] = a_ref[...]
     eye = (lax.broadcasted_iota(jnp.int32, (NB, NB), 0) == lax.broadcasted_iota(jnp.int32, (NB, NB), 1)).astype(jnp.float32)
-    up[...] = jnp.zeros_like(up)
     lane = lax.broadcasted_iota(jnp.int32, (1, NB), 1)
     sub_g = lax.broadcasted_iota(jnp.int32, (G, 1), 0)
     lane_g = lax.broadcasted_iota(jnp.int32, (G, NB), 1)
     for b in range(blocks):
         r0 = b * NB
-        dg[:, :NB] = work[r0:r0 + NB, r0:r0 + NB]
+        src = a_ref if b == 0 else work
+        dg[:, :NB] = src[r0:r0 + NB, r0:r0 + NB]
         dg[:, NB:] = eye
 
         def group(t, carry):
@@ -70,9 +69,9 @@
         up[r0:r0 + NB, r0:r0 + NB] = dg[:, :NB]
         inv[b] = dg[:, NB:]
         if b + 1 < blocks:
-            panel = _dot_nn(inv[b], work[r0:r0 + NB, r0 + NB:n])
+            panel = _dot_nn(inv[b], src[r0:r0 + NB, r0 + NB:n])
             up[r0:r0 + NB, r0 + NB:n] = panel
-            work[r0 + NB:n, r0 + NB:n] -= _dot_tn(panel, panel)
+            work[r0 + NB:n, r0 + NB:n] = src[r0 + NB:n, r0 + NB:n] - _dot_tn(panel, panel)
     rhs = r_ref[...]
     z = []
     for b in range(blocks):

time: 155 us -> 155 us (level)
  no operation moved by 1% of the time
where the time goes in v6:
time: 155 us; the launch traced here: 154 us
  blocking collectives  66 us (43%)
  Pallas kernels  53.7 us (35%)
  matrix products  16.9 us (11%)
  local copies, waits for them, and re-layouts  7.86 us (5%)
  other arithmetic  6.82 us (4%)
  between operations  2.7 us (2%)
    pallas_call x1, Pallas kernels, spd_solve(): pl.pallas_call(_solve_kernel, out_shape=jax.ShapeDtypeStruct(rhs.shape, j...  53.7 us
    all_gather x1, blocking collectives, on_device(): gathered = lax.all_gather(gathered, 'z', axis=0, tiled=True)  37.2 us
    all_gather x1, blocking collectives, on_device(): gathered = lax.all_gather(gathered, 'y', axis=0, tiled=True)  13.7 us
    all_gather x1, blocking collectives, on_device(): lax.all_gather(block_rows[:, :share], 'mp', axis=1, tiled=True)  13.3 us
    dot_general x1, matrix products, on_device(): lax.dot_general(block_points, points, (((1,), (1,)), ((), ())), precision...  7.25 us
    dot_general x1, matrix products, on_device(): jnp.dot(increment, weights, precision=highest, preferred_element_type=jnp...  4.16 us
    dot_general x1, matrix products, on_device(): jnp.dot(increment, placed, precision=highest, preferred_element_type=jnp....  3.27 us

profile of v6, /device:TPU:24, one launch (start us, length us, event | category | flops | bytes accessed | tf_op | source)
XLA Modules:
  0.0 154.1 jit_solution(2206792214712668273)
XLA Ops:
  0.6 0.6 compare_reduce_fusion
  1.3 0.7 broadcast_select_fusion.1
  2.0 0.2 convert_reduce_fusion
  2.2 0.1 select_reduce_fusion
  2.3 0.1 fusion.26
  2.5 2.7 %multiply_reduce_fusion = (f32[2048]{0:T(1024)S(1)}, f32[]{:T(128)}) fusion(f32[2048,256]{1,0:T(8,128)} %param.6), kind=kLoop, calls=%fused_computation.19 | loop fusion | flops 1570815 | bytes 2105348 | tf_op jit(solution)/shard_map/reduce_sum | solution.py:119
  6.6 2.2 %gather_fusion = f32[16,256]{1,0:T(8,128)S(1)} fusion(f32[2048,256]{1,0:T(8,128)} %param.6, s32[1024]{0:T(1024)S(1)} %pad_clamp_fusion.1), kind=kCustom, calls=%fused_computation | custom fusion | bytes 32832 | tf_op jit(solution)/shard_map/gather | solution.py:131
  8.8 1.3 copy.16
  10.1 0.6 gather_fusion.1
  10.8 1.8 %all-gather = f32[2,17,96]{2,1,0:T(8,128)S(1)} all-gather(f32[1,17,96]{2,1,0:T(8,128)S(1)} %fusion.27), channel_id=1, replica_groups=mesh['y'=4,'z'=16,'c'=2,'mp'=4] {'c'}, dimensions={0}, use_global_device_ids=true | all-gather | bytes 19584 | tf_op jit(solution)/shard_map/all_gather | solution.py:138
  12.6 37.2 %all-gather.1 = f32[16,34,96]{2,1,0:T(8,128)S(1)} all-gather(f32[1,34,96]{2,1,0:T(8,128)S(1)} %reshape.93), channel_id=1, replica_groups=mesh['y'=4,'z'=16,'c'=2,'mp'=4] {'z'}, dimensions={0}, use_global_device_ids=true | all-gather | bytes 221952 | tf_op jit(solution)/shard_map/all_gather | solution.py:139
  49.9 0.2 copy.17
  50.0 13.7 %all-gather.2 = f32[4,544,96]{1,2,0:T(8,128)S(1)} all-gather(f32[1,544,96]{1,2,0:T(8,128)S(1)} %copy.17), channel_id=1, replica_groups=mesh['y'=4,'z'=16,'c'=2,'mp'=4] {'y'}, dimensions={0}, use_global_device_ids=true | all-gather | bytes 1044480 | tf_op jit(solution)/shard_map/all_gather | solution.py:140
  63.7 0.4 copy.18
  64.1 1.0 gather_fusion.2
  65.4 0.7 copy.22
  66.2 13.3 %all_gather.15 = f32[512,256]{0,1:T(8,128)S(1)} all-gather(f32[512,64]{0,1:T(8,128)S(1)} %copy.19), channel_id=1, replica_groups=mesh['y'=4,'z'=16,'c'=2,'mp'=4] {'mp'}, dimensions={1}, use_global_device_ids=true | all-gather | bytes 655360 | tf_op jit(solution)/shard_map/all_gather | solution.py:143
  79.5 1.3 reshape.65
  80.8 1.9 %slice_reduce_fusion = f32[]{:T(128)} fusion(f32[128,17,96]{2,1,0:T(8,128)} %reshape.65), kind=kLoop, calls=%fused_computation.32 | loop fusion | flops 127 | bytes 516 | tf_op jit(solution)/shard_map/reduce_sum | solution.py:145
  83.4 2.3 %fusion.23.a_ref = f32[512,512]{1,0:T(8,128)} fusion(f32[512,256]{0,1:T(8,128)S(1)} %all_gather.15, f32[]{:T(128)S(6)} %div.31, f32[512]{0:T(512)S(1)} %multiply_reduce_fusion.2), kind=kOutput, calls=%fused_computation.26 | convolution fusion | flops 807403520 | bytes 1574916 | tf_op jit(solution)/shard_map/dot_general | solution.py:148
  85.6 53.7 %shard_map.59 = f32[32,512]{1,0:T(8,128)} custom-call(f32[512,512]{1,0:T(8,128)} %fusion.23.a_ref, f32[32,512]{1,0:T(8,128)} %bitcast.18), custom_call_target="tpu_custom_call" | custom-call | tf_op jit(solution)/shard_map/pallas_call | solution.py:93
  139.4 3.3 %fusion.32 = (f32[32,2048]{1,0:T(8,128)}, f32[32,2048]{1,0:T(8,128)S(1)}) fusion(f32[32,2048]{1,0:T(8,128)S(1)} %copy-done.3, f32[32,512]{1,0:T(8,128)} %shard_map.59, s32[512]{0:T(512)S(1)} %get-tuple-element.16), kind=kOutput, calls=%fused_computation.59 | convolution fusion | flops 403767296 | bytes 854016 | tf_op jit(solution)/shard_map/dot_general | solution.py:169
  142.6 7.2 %fusion.33 = f32[512,2048]{1,0:T(8,128)S(1)} fusion(f32[512,256]{0,1:T(8,128)S(1)} %all_gather.15, f32[2048,256]{1,0:T(8,128)S(1)} %copy-done), kind=kOutput, calls=%fused_computation.60 | convolution fusion | flops 3221225472 | bytes 6815744 | tf_op jit(solution)/shard_map/dot_general | solution.py:158
  149.9 4.2 %fusion.11 = f32[32,2048]{1,0:T(8,128)} fusion(f32[32,2048]{1,0:T(8,128)S(1)} %get-tuple-element.21, f32[32,2048]{1,0:T(8,128)S(1)} %copy-done.1, f32[32,512]{1,0:T(8,128)S(1)} %copy-done.2, f32[512,2048]{1,0:T(8,128)S(1)} %fusion.33, f32[]{:T(128)S(6)} %div.31, f32[2048]{0:T(1024)S(1)} %get-tuple-element.14, f32[512]{0:T(512)S(1)} %multiply_reduce_fusion.2), kind=kOutput, calls=%fused_computation.13 | convolution fusion | flops 408027136 | bytes 5056516 | tf_op jit(solution)/shard_map/dot_general | solution.py:166
  (20 shorter events, 0.6 us)
Async XLA Ops:
  79.5 59.8 %copy-start.3 = (f32[32,2048]{1,0:T(8,128)S(1)}, f32[32,2048]{1,0:T(8,128)}, u32[]{:S(2)}) copy-start(f32[32,2048]{1,0:T(8,128)} %param.8) | copy-start | bytes 786436
  80.8 61.9 %copy-start = (f32[2048,256]{1,0:T(8,128)S(1)}, f32[2048,256]{1,0:T(8,128)}, u32[]{:S(2)}) copy-start(f32[2048,256]{1,0:T(8,128)} %param.6) | copy-start | bytes 6291460
  139.4 10.5 %copy-start.1 = (f32[32,2048]{1,0:T(8,128)S(1)}, f32[32,2048]{1,0:T(8,128)}, u32[]{:S(2)}) copy-start(f32[32,2048]{1,0:T(8,128)} %param.7) | copy-start | bytes 786436
  139.4 10.5 %copy-start.2 = (f32[32,512]{1,0:T(8,128)S(1)}, f32[32,512]{1,0:T(8,128)}, u32[]{:S(2)}) copy-start(f32[32,512]{1,0:T(8,128)} %shard_map.59) | copy-start | bytes 196612
